TPU v7x, 256 devices: a whole 4x4x8 slice. The times are simulated.
256 devices in a mesh: ctx: 8 (over x, y_lo), chan: 32 (over z, y_hi, core).
Axes of the slice: x: 4, y: 4 (y_hi: 2, y_lo: 2; y = y_hi * 2 + y_lo), z: 8, core: 2. Of those that a mesh axis runs over, the one named last changes fastest.
Arguments:
- gate_input: bfloat16 [1024, 8192], P('ctx', 'chan'), may hold values from -6 to 6
- key_input: bfloat16 [1024, 8192], P('ctx', 'chan'), may hold values from -6 to 6
- value_input: bfloat16 [1024, 8192], P('ctx', 'chan'), may hold values from -6 to 6
- short_filters: float32 [3, 7, 8192], P(None, None, 'chan'), may hold values from -2.5 to 2.5
- pole_time: float32 [8192, 16], P('chan'), may hold values from 30 to 2048
- residues: float32 [8192, 16], P('chan'), may hold values from -1.5 to 1.5
- out_weight: bfloat16 [8192, 8192], P('ctx', 'chan'), may hold values from -0.125 to 0.125
- out_cotangent: bfloat16 [1024, 8192], P('ctx', 'chan'), may hold values from -6 to 6
Outputs:
- block_output: bfloat16 [1024, 8192], P('ctx', 'chan')
- gate_grad: bfloat16 [1024, 8192], P('ctx', 'chan')
- key_grad: bfloat16 [1024, 8192], P('ctx', 'chan')
- value_grad: bfloat16 [1024, 8192], P('ctx', 'chan')
All inputs are finite; a program needn't handle non-finite values.
Results may differ from a plain program's by a relative error of at most 0.0049.
Values may be sent and summed in bfloat16 or wider, within the bound.
No kernel may reach another device: no remote copies, remote signals or barrier semaphores. Data moves between devices by JAX's collectives and lax.ppermute only.
A program may use at most 64 MiB of HBM per device.

v0:
```python
import math
import jax
import jax.numpy as jnp
from jax import lax
from jax.sharding import PartitionSpec as P

HIGHEST = lax.Precision.HIGHEST


def from_behind(block, axis, distance):
    devices = range(lax.axis_size(axis))
    route = [(i - distance, i) for i in devices if i - distance in devices]
    return lax.ppermute(block, axis, route)


def carried_in(x, axis, combine, identity, reverse):
    peers, position = (lax.axis_size(axis), lax.axis_index(axis))
    everything = jax.tree.map(lambda part: lax.all_gather(part, axis), x)
    start = jax.tree.map(
        lambda part, zero: jnp.broadcast_to(jnp.asarray(zero, part.dtype), part.shape), x, identity
    )

    def lap(k, before):
        at = peers - 1 - k if reverse else k
        reached = at > position if reverse else at < position
        new = combine(before, jax.tree.map(lambda part: part[at], everything))
        return jax.tree.map(lambda a, b: jnp.where(reached, a, b), new, before)

    return lax.fori_loop(0, peers, lap, start)


def causal_taps(extended, filter_taps, length):
    tap_count = filter_taps.shape[0]
    summed = jnp.zeros((length, extended.shape[1]), jnp.float32)
    for offset in range(tap_count):
        lead_row = tap_count - 1 - offset
        summed = summed + filter_taps[offset][None, :] * extended[lead_row : lead_row + length]
    return summed


def anti_taps(extended, filter_taps, length):
    tap_count = filter_taps.shape[0]
    summed = jnp.zeros((length, extended.shape[1]), jnp.float32)
    for offset in range(tap_count):
        summed = summed + filter_taps[offset][None, :] * extended[offset : offset + length]
    return summed


def spectral_tables(length):
    doubled = 2 * length
    freqs = lax.broadcasted_iota(jnp.int32, (doubled, length), 0)
    places = lax.broadcasted_iota(jnp.int32, (doubled, length), 1)
    angles = (freqs * places % doubled).astype(jnp.float32) * (2.0 * math.pi / doubled)
    forward = jnp.concatenate([jnp.cos(angles), -jnp.sin(angles)], axis=0)
    inverse = forward.T / doubled
    return (forward, inverse)


def apply_filter(spectrum, signal, forward, inverse):
    middle = forward.shape[0] // 2
    spectra = jnp.dot(forward, signal, precision=HIGHEST)
    real_sig = spectra[:middle]
    imag_sig = spectra[middle:]
    real_filt = spectrum[:middle]
    imag_filt = spectrum[middle:]
    product = jnp.concatenate(
        [real_sig * real_filt - imag_sig * imag_filt, real_sig * imag_filt + imag_sig * real_filt],
        axis=0,
    )
    return jnp.dot(inverse, product, precision=HIGHEST)


def mode_sums(inv_time, modal_weight, mixed, grad_long, length):
    offsets = lax.broadcasted_iota(jnp.float32, (length, 1), 0)

    def one_mode(carry, pieces):
        rate_row, weight_row = pieces
        decay = jnp.exp(-offsets * rate_row[None, :])
        forward_sum = jnp.sum(decay[::-1] * mixed, axis=0)
        backward_sum = jnp.sum(decay * grad_long, axis=0)
        return (carry + weight_row[None, :] * decay, (forward_sum, backward_sum))

    start_filter = jnp.zeros((length, mixed.shape[1]), jnp.float32)
    filt_table, sums_pair = lax.scan(one_mode, start_filter, (inv_time, modal_weight))
    return (filt_table, sums_pair[0], sums_pair[1])


def mode_terms(inv_time, modal_weight, state_in, state_back, length):
    offsets = lax.broadcasted_iota(jnp.float32, (length, 1), 0)

    def one_mode(carry, pieces):
        rate_row, weight_row, enter_row, back_row = pieces
        decay = jnp.exp(-offsets * rate_row[None, :])
        step_decay = (weight_row * jnp.exp(-rate_row))[None, :]
        ahead = step_decay * decay * enter_row[None, :]
        behind = step_decay * decay[::-1] * back_row[None, :]
        return ((carry[0] + ahead, carry[1] + behind), None)

    start_terms = jnp.zeros((length, inv_time.shape[1]), jnp.float32)
    result_pair, _ = lax.scan(
        one_mode, (start_terms, start_terms), (inv_time, modal_weight, state_in, state_back)
    )
    return (result_pair[0], result_pair[1])


def chain_combine(earlier, later):
    return (earlier[0] * later[0], later[0] * earlier[1] + later[1])


def body(
    gate_input,
    key_input,
    value_input,
    short_filters,
    pole_time,
    residues,
    out_weight,
    out_cotangent,
):
    length = gate_input.shape[0]
    tap_count = short_filters.shape[1]
    stacked = jnp.stack([gate_input, key_input, value_input])
    tails = from_behind(stacked[:, length - (tap_count - 1) :, :], "ctx", 1)
    extended = jnp.concatenate([tails, stacked], axis=1).astype(jnp.float32)
    gate_short = causal_taps(extended[0], short_filters[0], length)
    key_short = causal_taps(extended[1], short_filters[1], length)
    value_short = causal_taps(extended[2], short_filters[2], length)
    mixed = key_short * value_short
    weight_full = lax.all_gather(out_weight, "ctx", axis=0, tiled=True)
    row_block = weight_full
    grad_gated = lax.psum_scatter(
        lax.dot_general(
            row_block, out_cotangent, (((1,), (1,)), ((), ())), preferred_element_type=jnp.float32
        ),
        "chan",
        scatter_dimension=0,
        tiled=True,
    ).T
    grad_long = grad_gated * gate_short
    inv_time = 1.0 / pole_time.T
    modal_weight = residues.T * jnp.sqrt(-jnp.expm1(-2.0 * inv_time))
    filt_table, forward_sums, backward_sums = mode_sums(
        inv_time, modal_weight, mixed, grad_long, length
    )
    block_decay = jnp.exp(-float(length) * inv_time)
    identity = (jnp.ones_like(block_decay), jnp.zeros_like(block_decay))
    state_in = carried_in((block_decay, forward_sums), "ctx", chain_combine, identity, False)[1]
    state_back = carried_in((block_decay, backward_sums), "ctx", chain_combine, identity, True)[1]
    forward, inverse = spectral_tables(length)
    spectrum = jnp.dot(forward, filt_table, precision=HIGHEST)
    long_local = apply_filter(spectrum, mixed, forward, inverse)
    back_local = apply_filter(spectrum, grad_long[::-1], forward, inverse)[::-1]
    ahead_terms, behind_terms = mode_terms(inv_time, modal_weight, state_in, state_back, length)
    long_out = long_local + ahead_terms
    grad_mixed = back_local + behind_terms
    gated = (gate_short * long_out).astype(jnp.bfloat16)
    row_block = weight_full
    block_output = jnp.dot(
        lax.all_gather(gated, "chan", axis=1, tiled=True),
        row_block,
        preferred_element_type=jnp.float32,
    ).astype(jnp.bfloat16)
    grad_gate_short = grad_gated * long_out
    grad_key_short = grad_mixed * value_short
    grad_value_short = grad_mixed * key_short
    grads = jnp.stack([grad_gate_short, grad_key_short, grad_value_short])
    heads = from_behind(grads[:, : tap_count - 1, :], "ctx", -1)
    ext_grads = jnp.concatenate([grads, heads], axis=1)
    gate_grad = anti_taps(ext_grads[0], short_filters[0], length).astype(jnp.bfloat16)
    key_grad = anti_taps(ext_grads[1], short_filters[1], length).astype(jnp.bfloat16)
    value_grad = anti_taps(ext_grads[2], short_filters[2], length).astype(jnp.bfloat16)
    return (block_output, gate_grad, key_grad, value_grad)


def solution(mesh):
    in_specs = (
        P("ctx", "chan"),
        P("ctx", "chan"),
        P("ctx", "chan"),
        P(None, None, "chan"),
        P("chan", None),
        P("chan", None),
        P("ctx", "chan"),
        P("ctx", "chan"),
    )
    out_specs = (P("ctx", "chan"), P("ctx", "chan"), P("ctx", "chan"), P("ctx", "chan"))
    return jax.shard_map(body, mesh=mesh, in_specs=in_specs, out_specs=out_specs, check_vma=False)
```

profile of v0, /device:TPU:1, one launch (start us, length us, event | category | flops | bytes accessed | tf_op | source)
XLA Modules:
  0.0 426.2 jit_solution(3915547119389081948)
XLA Ops:
  7.2 0.7 all-gather.6.cloned.1.call-update
  8.0 97.7 %all-gather.6.cloned.1.call-done = bf16[8192,256]{1,0:T(8,128)(2,1)} async-done(((bf16[1024,256]{1,0:T(8,128)(2,1)}), bf16[8192,256]{1,0:T(8,128)(2,1)}) %all-gather.6.cloned.1.call-update) | async-done | bytes 4194320 | tf_op jit(solution)/shard_map/all_gather | solution.py:129
  105.7 5.5 %fusion.119 = f32[8192,128]{1,0:T(8,128)} fusion(bf16[8192,256]{1,0:T(8,128)(2,1)} %all-gather.6.cloned.1.call-done, bf16[128,256]{1,0:T(8,128)(2,1)S(1)} %copy-done), kind=kOutput, calls=%fused_computation.197 | convolution fusion | flops 536870912 | bytes 8454144 | tf_op jit(solution)/shard_map/dot_general | solution.py:132
  111.2 0.7 copy-done.3
  112.3 0.1 pad_maximum_fusion.4
  112.5 1.5 collective-permute-start
  114.0 0.5 sine_negate_fusion
  114.6 25.4 %all-gather = f32[128,256]{1,0:T(8,128)} all-gather(f32[16,256]{1,0:T(8,128)S(1)} %get-tuple-element.639), channel_id=2, replica_groups=mesh['ctx'=8,'chan'=32] {'ctx'}, dimensions={0}, use_global_device_ids=true | all-gather | bytes 147456 | tf_op jit(solution)/shard_map/all_gather | solution.py:18
  140.1 0.2 maximum_convert_fusion
  140.3 0.9 fusion.114
  141.3 0.6 fusion.103
  141.9 93.7 %reduce-scatter.2.cloned.1.call-done = f32[256,128]{1,0:T(8,128)} async-done(((f32[8192,128]{1,0:T(8,128)}), f32[256,128]{1,0:T(8,128)}) %reduce-scatter.2.cloned.1.call-update) | async-done | bytes 131088 | tf_op jit(solution)/shard_map/reduce_scatter | solution.py:131
  235.6 2.1 bitcast_multiply_fusion.3
  237.6 0.2 rev.16
  237.9 0.6 fusion.101
  238.5 6.3 %while.62 = (s32[]{:T(128)}, f32[128,256]{1,0:T(8,128)S(1)}, f32[16,256]{1,0:T(8,128)S(1)}, f32[16,256]{1,0:T(8,128)S(1)}, f32[16,256]{1,0:T(8,128)S(1)}, /*inde...) while((s32[]{:T(128)}, f32[128,256]{1,0:T(8,128)S(1)}, ...), condition=%wide.region_4.5_spmd.clone, body=%wide.region_1.4_spmd.clone.sunk | while | flops 261763 | bytes 1062019 | solution.py:84
  238.6 0.1 multiply_reduce_fusion.4
  239.0 0.1 multiply_reduce_fusion.4
  239.4 0.1 multiply_reduce_fusion.4
  239.7 0.1 multiply_reduce_fusion.4
  240.1 0.1 multiply_reduce_fusion.4
  240.5 0.1 multiply_reduce_fusion.4
  241.3 0.1 multiply_reduce_fusion.4
  241.7 0.1 multiply_reduce_fusion.4
  242.1 0.1 multiply_reduce_fusion.4
  242.5 0.1 multiply_reduce_fusion.4
  242.9 0.1 multiply_reduce_fusion.4
  244.1 0.1 multiply_reduce_fusion.4
  244.5 0.1 multiply_reduce_fusion.4
  244.8 0.6 fusion.102
  245.5 1.0 fusion.9
  246.5 0.2 rev.17
  246.7 21.8 %all-gather.1 = f32[128,256]{1,0:T(8,128)S(1)} all-gather(f32[16,256]{1,0:T(8,128)S(1)} %get-tuple-element.433), channel_id=3, replica_groups=mesh['ctx'=8,'chan'=32] {'ctx'}, dimensions={0}, use_global_device_ids=true | all-gather | bytes 147456 | tf_op jit(solution)/shard_map/all_gather | solution.py:18
  268.6 5.8 %while.63 = (s32[]{:T(128)}, f32[16,256]{1,0:T(8,128)S(1)}, s32[]{:T(128)}, f32[8,16,256]{2,1,0:T(8,128)}, f32[8,16,256]{2,1,0:T(8,128)S(1)}, /*index=5*/s32[]{:T(128)}, s32[]{:T(128)}) while((s32[]{:T(128)}, f32[16,256]{1,0:T(8,128)S(1)}, s32[]{:T(128)}, f32[8,16,256]{2,1,0:T(8,128)}, f32[8,16,256]{2,1,0:T(8,128)S(1)}, ...), condition=%wide.region_6.7_spmd.clone, body=%wide.region_5.6_spmd.clone.sunk | while | flops 16388 | bytes 65645 | solution.py:29
  268.6 0.7 fusion.129
  269.3 0.7 fusion.129
  270.0 0.7 fusion.129
  270.7 0.7 fusion.129
  271.5 0.7 fusion.129
  272.2 0.7 fusion.129
  272.9 0.7 fusion.129
  273.6 0.7 fusion.129
  274.4 21.8 %all-gather.2 = f32[128,256]{1,0:T(8,128)S(1)} all-gather(f32[16,256]{1,0:T(8,128)S(1)} %get-tuple-element.435), channel_id=4, replica_groups=mesh['ctx'=8,'chan'=32] {'ctx'}, dimensions={0}, use_global_device_ids=true | all-gather | bytes 147456 | tf_op jit(solution)/shard_map/all_gather | solution.py:18
  296.2 5.8 %while.64 = (s32[]{:T(128)}, f32[16,256]{1,0:T(8,128)S(1)}, s32[]{:T(128)}, f32[8,16,256]{2,1,0:T(8,128)}, f32[8,16,256]{2,1,0:T(8,128)S(1)}, /*index=5*/s32[]{:T(128)}, s32[]{:T(128)}, s32[]{:T(128)}, s32[]{:T(128)}) while((s32[]{:T(128)}, f32[16,256]{1,0:T(8,128)S(1)}, s32[]{:T(128)}, f32[8,16,256]{2,1,0:T(8,128)}, ...), condition=%wide.region_8.9_spmd.clone, body=%wide.region_7.8_spmd.clone.sunk | while | flops 16392 | bytes 65707 | solution.py:29
  296.2 0.7 fusion.130
  296.9 0.7 fusion.130
  297.6 0.7 fusion.130
  298.3 0.7 fusion.130
  299.1 0.7 fusion.130
  299.8 0.7 fusion.130
  300.5 0.7 fusion.130
  301.2 0.7 fusion.130
  302.0 5.4 %while.65 = (s32[]{:T(128)}, f32[128,256]{1,0:T(8,128)S(1)}, f32[128,256]{1,0:T(8,128)S(1)}, f32[16,256]{1,0:T(8,128)S(1)}, f32[16,256]{1,0:T(8,128)S(1)}, /*ind...) while((s32[]{:T(128)}, f32[128,256]{1,0:T(8,128)S(1)}, ...), condition=%wide.region_10.11_spmd.clone, body=%wide.region_9.10_spmd.clone.sunk | while | flops 295555 | bytes 1063032 | solution.py:100
  307.6 1.0 convolution_add_fusion
  308.7 1.3 collective-permute-start.1
  310.0 7.3 %collective-permute-done.1 = f32[3,6,256]{1,2,0:T(8,128)S(1)} collective-permute-done((f32[3,6,256]{1,2,0:T(8,128)S(1)}, f32[3,6,256]{1,2,0:T(8,128)S(1)}, u32[]{:S(2)}, u32[]{:S(2)}) %collective-permute-start.1) | collective-permute-done | bytes 18464 | tf_op jit(solution)/shard_map/ppermute | solution.py:13
  317.4 1.1 fusion.46
  318.5 0.7 copy.21
  319.2 0.5 fusion.33
  319.7 0.7 copy.22
  320.5 0.5 fusion.20
  321.0 0.7 copy.23
  321.7 93.5 %all-gather.8.cloned.1.call-done = bf16[128,8192]{0,1:T(8,128)(2,1)} async-done(((bf16[128,256]{0,1:T(8,128)(2,1)}), bf16[128,8192]{0,1:T(8,128)(2,1)}) %all-gather.8.cloned.1.call-update) | async-done | bytes 2097168 | tf_op jit(solution)/shard_map/all_gather | solution.py:159
  415.2 4.4 %convolution_convert_fusion = bf16[128,256]{1,0:T(8,128)(2,1)} fusion(bf16[128,8192]{0,1:T(8,128)(2,1)} %all-gather.8.cloned.1.call-done, bf16[8192,256]{1,0:T(8,128)(2,1)} %all-gather.6.cloned.1.call-done), kind=kOutput, calls=%fused_computation.24 | convolution fusion | flops 536903680 | bytes 6356992 | tf_op jit(solution)/shard_map/dot_general | solution.py:158
  (242 shorter events, 9.5 us)
Async XLA Ops:
  7.2 98.5 %copy-start = (bf16[128,256]{1,0:T(8,128)(2,1)S(1)}, bf16[128,256]{1,0:T(8,128)(2,1)}, u32[]{:S(2)}) copy-start(bf16[128,256]{1,0:T(8,128)(2,1)} %param.23) | copy-start | bytes 196612
  7.2 98.5 %all-gather.6.cloned.1.call-start = ((), (), s32[]{:S(2)}) async-start(), calls=%async_computation.1 | async-start | bytes 4718592 | tf_op jit(solution)/shard_map/all_gather | solution.py:129
  7.9 227.7 %reduce-scatter.2.cloned.1.call-start = ((), (), s32[]{:S(2)}) async-start(), calls=%async_computation.2 | async-start | bytes 4325376 | tf_op jit(solution)/shard_map/reduce_scatter | solution.py:131
  111.1 0.8 copy-start.3
  111.1 1.0 copy-start.4
  111.1 1.1 copy-start.5
  111.1 3.4 copy-start.7
  111.1 3.4 copy-start.6
  111.1 3.4 copy-start.8
  111.2 304.0 %all-gather.8.cloned.1.call-start = ((), (), s32[]{:S(2)}) async-start(), calls=%async_computation.3 | async-start | bytes 2162688 | tf_op jit(solution)/shard_map/all_gather | solution.py:159
  112.5 27.6 %collective-permute-start = (bf16[3,6,256]{1,2,0:T(8,128)(2,1)S(1)}, bf16[3,6,256]{1,2,0:T(8,128)(2,1)S(1)}, u32[]{:S(2)}, u32[]{:S(2)}) collective-permute-start(bf16[3,6,256]{1,2,0:T(8,128)(2,1)S(1)} %pad_maximum_fusion.4), channel_id=1, source_target_pairs={{0,32},{32,64},{64,96},{96,128},{128,160},{160,192},{192,224},{1,3... | collective-permute-start | bytes 27656 | tf_op jit(solution)/shard_map/ppermute | solution.py:13
  301.9 6.6 %copy-start.1 = (f32[256,128]{1,0:T(8,128)S(1)}, f32[256,128]{1,0:T(8,128)}, u32[]{:S(2)}) copy-start(f32[256,128]{1,0:T(8,128)} %reduce-scatter.2.cloned.1.call-done) | copy-start | bytes 393220
  302.0 15.4 %copy-start.2 = (f32[128,256]{0,1:T(8,128)S(1)}, f32[128,256]{0,1:T(8,128)}, u32[]{:S(2)}) copy-start(f32[128,256]{0,1:T(8,128)} %get-tuple-element.595) | copy-start | bytes 393220
  308.7 8.6 %collective-permute-start.1 = (f32[3,6,256]{1,2,0:T(8,128)S(1)}, f32[3,6,256]{1,2,0:T(8,128)S(1)}, u32[]{:S(2)}, u32[]{:S(2)}) collective-permute-start(f32[3,6,256]{1,2,0:T(8,128)S(1)} %pad_maximum_fusion.1), channel_id=1, source_target_pairs={{32,0},{64,32},{96,64},{128,96},{160,128},{192,160},{224,192},{33,... | collective-permute-start | bytes 55304 | tf_op jit(solution)/shard_map/ppermute | solution.py:13
Sparse Core Ops, SparseCore 0:
  9.8 95.8 all-gather.5
  111.3 124.2 reduce-scatter.1
  318.6 96.5 all-gather.7
where the time goes:
time: 428 us; the launch traced here: 426 us
  waiting for transfers between devices  293 us (68%)
  blocking collectives  69 us (16%)
  other arithmetic  23.4 us (5%)
  between operations  14.1 us (3%)
  matrix products  13.6 us (3%)
  local copies, waits for them, and re-layouts  8.38 us (2%)
    all_gather x1, waiting for transfers between devices, body(): weight_full = lax.all_gather(out_weight, 'ctx', axis=0, tiled=True)  97.7 us
    reduce_scatter x1, waiting for transfers between devices, body(): lax.psum_scatter(lax.dot_general(row_block, out_cotangent, (((1,), (1,)),...  93.7 us
    all_gather x1, waiting for transfers between devices, body(): lax.all_gather(gated, 'chan', axis=1, tiled=True)  93.5 us
    all_gather x3, blocking collectives, carried_in(): everything = jax.tree.map(lambda part: lax.all_gather(part, axis), x)  69 us
    select_n x16, other arithmetic, lap(): return jax.tree.map(lambda a, b: jnp.where(reached, a, b), new, before)  11.6 us
  transfers between devices with their start and end apart: 5, of which 4 were waited for; matrix products, arithmetic and copies ran while one was open for 1% of the time, Pallas kernels for 0%

commit v1 on v0

--- a/solution.py
+++ b/solution.py
@@ -3,6 +3,7 @@
 import jax.numpy as jnp
 from jax import lax
 from jax.sharding import PartitionSpec as P
+from jax.lax import all_to_all, axis_size
 
 HIGHEST = lax.Precision.HIGHEST
 
@@ -156,7 +157,7 @@
     gated = (gate_short * long_out).astype(jnp.bfloat16)
     row_block = weight_full
     block_output = jnp.dot(
-        lax.all_gather(gated, "chan", axis=1, tiled=True),
+        jnp.concatenate(all_to_all(jnp.stack([gated] * axis_size("chan")), "chan", 0, 0), axis=1),
         row_block,
         preferred_element_type=jnp.float32,
     ).astype(jnp.bfloat16)

time: 428 us -> 416 us (0.972)
  waiting for transfers between devices: 293 us -> 247 us
  starting transfers between devices: 2.91 us -> 28.3 us
  local copies, waits for them, and re-layouts: 8.38 us -> 30.8 us
  other arithmetic: 23.4 us -> 11.3 us
    all_gather x1 -> x0, waiting for transfers between devices: 93.5 us -> none  [body(): lax.all_gather(gated, 'chan', axis=1, tiled=True)]
    all_to_all x0 -> x1, waiting for transfers between devices: none -> 46.1 us  [body(): all_to_all(jnp.stack([gated] * axis_size('chan')), 'chan', 0, 0)]
    all_to_all x0 -> x1, starting transfers between devices: none -> 25.4 us  [body(): all_to_all(jnp.stack([gated] * axis_size('chan')), 'chan', 0, 0)]
    dynamic_update_slice x32, local copies, waits for them, and re-layouts: 1.36 us -> 21.7 us  [mode_sums(): lax.scan(one_mode, start_filter, (inv_time, modal_weight))]
    select_n x16, other arithmetic: 11.6 us -> 0.18 us  [lap(): return jax.tree.map(lambda a, b: jnp.where(reached, a, b), new, before)]
  transfers between devices with their start and end apart: 5 -> 5, of which waited for: 4 -> 4; matrix products, arithmetic and copies ran while one was open for 1% -> 2% of each run, Pallas kernels for 0% -> 0%
where the time goes in v1:
time: 416 us; the launch traced here: 414 us
  waiting for transfers between devices  247 us (59%)
  blocking collectives  66.8 us (16%)
  local copies, waits for them, and re-layouts  30.8 us (7%)
  starting transfers between devices  28.3 us (7%)
  between operations  15 us (4%)
  matrix products  13 us (3%)
  other arithmetic  11.3 us (3%)
    all_gather x1, waiting for transfers between devices, body(): weight_full = lax.all_gather(out_weight, 'ctx', axis=0, tiled=True)  97.7 us
    reduce_scatter x1, waiting for transfers between devices, body(): lax.psum_scatter(lax.dot_general(row_block, out_cotangent, (((1,), (1,)),...  95.6 us
    all_gather x3, blocking collectives, carried_in(): everything = jax.tree.map(lambda part: lax.all_gather(part, axis), x)  66.8 us
    all_to_all x1, waiting for transfers between devices, body(): all_to_all(jnp.stack([gated] * axis_size('chan')), 'chan', 0, 0)  46.1 us
    all_to_all x1, starting transfers between devices, body(): all_to_all(jnp.stack([gated] * axis_size('chan')), 'chan', 0, 0)  25.4 us
    dynamic_update_slice x32, local copies, waits for them, and re-layouts, mode_sums(): lax.scan(one_mode, start_filter, (inv_time, modal_weight))  21.7 us
  transfers between devices with their start and end apart: 5, of which 4 were waited for; matrix products, arithmetic and copies ran while one was open for 2% of the time, Pallas kernels for 0%

profile of v1, /device:TPU:1, one launch (start us, length us, event | category | flops | bytes accessed | tf_op | source)
XLA Modules:
  0.0 414.4 jit_solution(10993899141801166496)
XLA Ops:
  7.2 0.7 all-gather.5.cloned.1.call-update
  8.0 97.7 %all-gather.5.cloned.1.call-done = bf16[8192,256]{1,0:T(8,128)(2,1)} async-done(((bf16[1024,256]{1,0:T(8,128)(2,1)}), bf16[8192,256]{1,0:T(8,128)(2,1)}) %all-gather.5.cloned.1.call-update) | async-done | bytes 4194320 | tf_op jit(solution)/shard_map/all_gather | solution.py:130
  105.7 5.5 %fusion.119 = f32[8192,128]{1,0:T(8,128)} fusion(bf16[8192,256]{1,0:T(8,128)(2,1)} %all-gather.5.cloned.1.call-done, bf16[128,256]{1,0:T(8,128)(2,1)S(1)} %copy-done), kind=kOutput, calls=%fused_computation.197 | convolution fusion | flops 536870912 | bytes 8454144 | tf_op jit(solution)/shard_map/dot_general | solution.py:133
  111.2 0.8 copy-done.2
  112.3 0.1 pad_maximum_fusion.4
  112.4 1.5 collective-permute-start
  114.0 0.5 sine_negate_fusion
  114.8 23.1 %all-gather = f32[128,256]{1,0:T(8,128)S(1)} all-gather(f32[16,256]{1,0:T(8,128)S(1)} %get-tuple-element.651), channel_id=2, replica_groups=mesh['ctx'=8,'chan'=32] {'ctx'}, dimensions={0}, use_global_device_ids=true | all-gather | bytes 147456 | tf_op jit(solution)/shard_map/all_gather | solution.py:19
  138.0 0.2 maximum_convert_fusion
  138.2 0.9 fusion.114
  139.4 0.6 fusion.103
  139.9 95.6 %reduce-scatter.2.cloned.1.call-done = f32[256,128]{1,0:T(8,128)} async-done(((f32[8192,128]{1,0:T(8,128)}), f32[256,128]{1,0:T(8,128)}) %reduce-scatter.2.cloned.1.call-update) | async-done | bytes 131088 | tf_op jit(solution)/shard_map/reduce_scatter | solution.py:132
  235.6 1.4 bitcast_multiply_fusion.3
  237.0 0.2 rev.16
  237.3 0.6 fusion.101
  237.9 26.1 %while.62 = (s32[]{:T(128)}, f32[128,256]{1,0:T(8,128)S(1)}, f32[16,256]{1,0:T(8,128)S(1)}, f32[16,256]{1,0:T(8,128)}, f32[16,256]{1,0:T(8,128)S(1)}, /*index=5*...) while((s32[]{:T(128)}, f32[128,256]{1,0:T(8,128)S(1)}, ...), condition=%wide.region_4.5_spmd.clone, body=%wide.region_1.4_spmd.clone.sunk | while | flops 261763 | bytes 1062019 | solution.py:85
  238.0 0.1 multiply_reduce_fusion.4
  238.3 1.3 dynamic_update_slice.16
  239.6 0.1 multiply_reduce_fusion.4
  239.9 1.3 dynamic_update_slice.16
  241.2 0.1 multiply_reduce_fusion.4
  241.5 1.3 dynamic_update_slice.16
  242.9 0.1 multiply_reduce_fusion.4
  243.2 1.3 dynamic_update_slice.16
  244.5 0.1 multiply_reduce_fusion.4
  244.8 1.3 dynamic_update_slice.16
  246.1 0.1 multiply_reduce_fusion.4
  246.4 1.3 dynamic_update_slice.16
  247.8 0.1 multiply_reduce_fusion.4
  248.1 1.3 dynamic_update_slice.16
  249.7 1.3 dynamic_update_slice.16
  251.3 1.3 dynamic_update_slice.16
  252.7 0.1 multiply_reduce_fusion.4
  253.0 1.3 dynamic_update_slice.16
  254.6 1.3 dynamic_update_slice.16
  255.9 0.1 multiply_reduce_fusion.4
  256.2 1.3 dynamic_update_slice.16
  257.8 1.3 dynamic_update_slice.16
  259.5 1.3 dynamic_update_slice.16
  260.8 0.1 multiply_reduce_fusion.4
  261.1 1.3 dynamic_update_slice.16
  262.7 1.3 dynamic_update_slice.16
  264.1 0.6 fusion.102
  264.6 0.1 multiply_subtract_fusion
  264.8 1.0 fusion.9
  265.8 0.2 rev.17
  265.9 21.8 %all-gather.1 = f32[128,256]{1,0:T(8,128)S(1)} all-gather(f32[16,256]{1,0:T(8,128)S(1)} %get-tuple-element.433), channel_id=3, replica_groups=mesh['ctx'=8,'chan'=32] {'ctx'}, dimensions={0}, use_global_device_ids=true | all-gather | bytes 147456 | tf_op jit(solution)/shard_map/all_gather | solution.py:19
  287.8 0.3 while.63
  288.1 21.9 %all-gather.2 = f32[128,256]{1,0:T(8,128)S(1)} all-gather(f32[16,256]{1,0:T(8,128)S(1)} %copy-done.7), channel_id=4, replica_groups=mesh['ctx'=8,'chan'=32] {'ctx'}, dimensions={0}, use_global_device_ids=true | all-gather | bytes 147456 | tf_op jit(solution)/shard_map/all_gather | solution.py:19
  309.9 0.3 while.64
  310.4 5.4 %while.65 = (s32[]{:T(128)}, f32[128,256]{1,0:T(8,128)S(1)}, f32[128,256]{1,0:T(8,128)S(1)}, f32[16,256]{1,0:T(8,128)S(1)}, f32[16,256]{1,0:T(8,128)S(1)}, /*ind...) while((s32[]{:T(128)}, f32[128,256]{1,0:T(8,128)S(1)}, ...), condition=%wide.region_10.11_spmd.clone, body=%wide.region_9.10_spmd.clone.sunk | while | flops 295555 | bytes 1063032 | solution.py:101
  316.0 1.0 convolution_add_fusion
  317.1 1.3 collective-permute-start.1
  318.4 7.4 %collective-permute-done.1 = f32[3,6,256]{1,2,0:T(8,128)S(1)} collective-permute-done((f32[3,6,256]{1,2,0:T(8,128)S(1)}, f32[3,6,256]{1,2,0:T(8,128)S(1)}, u32[]{:S(2)}, u32[]{:S(2)}) %collective-permute-start.1) | collective-permute-done | bytes 18464 | tf_op jit(solution)/shard_map/ppermute | solution.py:14
  325.9 0.5 fusion.46
  326.5 1.8 stack.22
  328.3 25.4 %all-to-all-start = ((bf16[32,128,256]{1,2,0:T(8,128)(2,1)}), bf16[32,128,256]{1,2,0:T(8,128)(2,1)S(1)}, u32[]{:S(2)}, u32[]{:S(2)}) async-start(bf16[32,128,256]{1,2,0:T(8,128)(2,1)} %stack.22), calls=%async_computation.1 | async-start | bytes 4194304 | tf_op jit(solution)/shard_map/all_to_all | solution.py:160
  353.7 0.7 copy.34
  354.5 1.2 fusion.33
  355.7 0.7 copy.35
  356.4 0.5 fusion.20
  357.0 0.7 copy.36
  357.7 46.1 %all-to-all-done = bf16[32,128,256]{1,2,0:T(8,128)(2,1)S(1)} async-done(((bf16[32,128,256]{1,2,0:T(8,128)(2,1)}), bf16[32,128,256]{1,2,0:T(8,128)(2,1)S(1)}, u32[]{:S(2)}, u32[]{:S(2)}) %all-to-all-start) | async-done | bytes 2097184 | tf_op jit(solution)/shard_map/all_to_all | solution.py:160
  403.8 3.8 convolution_convert_fusion
  (320 shorter events, 9.3 us)
Async XLA Ops:
  7.2 98.5 %copy-start = (bf16[128,256]{1,0:T(8,128)(2,1)S(1)}, bf16[128,256]{1,0:T(8,128)(2,1)}, u32[]{:S(2)}) copy-start(bf16[128,256]{1,0:T(8,128)(2,1)} %param.23) | copy-start | bytes 196612
  7.2 98.5 %all-gather.5.cloned.1.call-start = ((), (), s32[]{:S(2)}) async-start(), calls=%async_computation.2 | async-start | bytes 4718592 | tf_op jit(solution)/shard_map/all_gather | solution.py:130
  7.9 227.7 %reduce-scatter.2.cloned.1.call-start = ((), (), s32[]{:S(2)}) async-start(), calls=%async_computation.3 | async-start | bytes 4325376 | tf_op jit(solution)/shard_map/reduce_scatter | solution.py:132
  111.1 0.8 copy-start.2
  111.1 1.0 copy-start.3
  111.1 1.1 copy-start.4
  111.1 3.4 copy-start.6
  111.1 3.5 copy-start.5
  111.1 3.7 copy-start.8
  112.4 25.5 %collective-permute-start = (bf16[3,6,256]{1,2,0:T(8,128)(2,1)S(1)}, bf16[3,6,256]{1,2,0:T(8,128)(2,1)S(1)}, u32[]{:S(2)}, u32[]{:S(2)}) collective-permute-start(bf16[3,6,256]{1,2,0:T(8,128)(2,1)S(1)} %pad_maximum_fusion.4), channel_id=1, source_target_pairs={{0,32},{32,64},{64,96},{96,128},{128,160},{160,192},{192,224},{1,3... | collective-permute-start | bytes 27656 | tf_op jit(solution)/shard_map/ppermute | solution.py:14
  114.5 24.7 %copy-start.30 = (f32[1,1,256]{2,1,0:T(1,128)}, f32[1,1,256]{2,1,0:T(1,128)S(1)}, u32[]{:S(2)}) copy-start(f32[1,1,256]{2,1,0:T(1,128)S(1)} %get-tuple-element.649) | copy-start | bytes 3076
  114.5 24.7 %copy-start.32 = (f32[1,1,256]{2,1,0:T(1,128)}, f32[1,1,256]{2,1,0:T(1,128)S(1)}, u32[]{:S(2)}) copy-start(f32[1,1,256]{2,1,0:T(1,128)S(1)} %get-tuple-element.650) | copy-start | bytes 3076
  114.6 24.7 %copy-start.9 = (f32[1,1,256]{2,1,0:T(1,128)}, f32[1,1,256]{2,1,0:T(1,128)S(1)}, u32[]{:S(2)}) copy-start(f32[1,1,256]{2,1,0:T(1,128)S(1)} %get-tuple-element.631) | copy-start | bytes 3076
  114.6 24.7 %copy-start.11 = (f32[1,1,256]{2,1,0:T(1,128)}, f32[1,1,256]{2,1,0:T(1,128)S(1)}, u32[]{:S(2)}) copy-start(f32[1,1,256]{2,1,0:T(1,128)S(1)} %get-tuple-element.632) | copy-start | bytes 3076
  114.6 24.7 %copy-start.13 = (f32[1,1,256]{2,1,0:T(1,128)}, f32[1,1,256]{2,1,0:T(1,128)S(1)}, u32[]{:S(2)}) copy-start(f32[1,1,256]{2,1,0:T(1,128)S(1)} %get-tuple-element.633) | copy-start | bytes 3076
  114.6 24.7 %copy-start.15 = (f32[1,1,256]{2,1,0:T(1,128)}, f32[1,1,256]{2,1,0:T(1,128)S(1)}, u32[]{:S(2)}) copy-start(f32[1,1,256]{2,1,0:T(1,128)S(1)} %get-tuple-element.634) | copy-start | bytes 3076
  114.6 24.7 %copy-start.17 = (f32[1,1,256]{2,1,0:T(1,128)}, f32[1,1,256]{2,1,0:T(1,128)S(1)}, u32[]{:S(2)}) copy-start(f32[1,1,256]{2,1,0:T(1,128)S(1)} %get-tuple-element.635) | copy-start | bytes 3076
  114.6 24.7 %copy-start.19 = (f32[1,1,256]{2,1,0:T(1,128)}, f32[1,1,256]{2,1,0:T(1,128)S(1)}, u32[]{:S(2)}) copy-start(f32[1,1,256]{2,1,0:T(1,128)S(1)} %get-tuple-element.630) | copy-start | bytes 3076
  114.6 24.7 %copy-start.21 = (f32[1,1,256]{2,1,0:T(1,128)}, f32[1,1,256]{2,1,0:T(1,128)S(1)}, u32[]{:S(2)}) copy-start(f32[1,1,256]{2,1,0:T(1,128)S(1)} %get-tuple-element.636) | copy-start | bytes 3076
  114.6 24.7 %copy-start.23 = (f32[1,1,256]{2,1,0:T(1,128)}, f32[1,1,256]{2,1,0:T(1,128)S(1)}, u32[]{:S(2)}) copy-start(f32[1,1,256]{2,1,0:T(1,128)S(1)} %get-tuple-element.637) | copy-start | bytes 3076
  114.7 24.7 %copy-start.25 = (f32[1,1,256]{2,1,0:T(1,128)}, f32[1,1,256]{2,1,0:T(1,128)S(1)}, u32[]{:S(2)}) copy-start(f32[1,1,256]{2,1,0:T(1,128)S(1)} %get-tuple-element.638) | copy-start | bytes 3076
  114.7 24.7 %copy-start.27 = (f32[1,1,256]{2,1,0:T(1,128)}, f32[1,1,256]{2,1,0:T(1,128)S(1)}, u32[]{:S(2)}) copy-start(f32[1,1,256]{2,1,0:T(1,128)S(1)} %get-tuple-element.639) | copy-start | bytes 3076
  114.7 24.7 %copy-start.28 = (f32[1,1,256]{2,1,0:T(1,128)}, f32[1,1,256]{2,1,0:T(1,128)S(1)}, u32[]{:S(2)}) copy-start(f32[1,1,256]{2,1,0:T(1,128)S(1)} %get-tuple-element.640) | copy-start | bytes 3076
  114.7 24.7 %copy-start.29 = (f32[1,1,256]{2,1,0:T(1,128)}, f32[1,1,256]{2,1,0:T(1,128)S(1)}, u32[]{:S(2)}) copy-start(f32[1,1,256]{2,1,0:T(1,128)S(1)} %get-tuple-element.641) | copy-start | bytes 3076
  114.7 122.5 %copy-start.34 = (f32[1,1,256]{2,1,0:T(1,128)}, f32[1,1,256]{2,1,0:T(1,128)S(1)}, u32[]{:S(2)}) copy-start(f32[1,1,256]{2,1,0:T(1,128)S(1)} %get-tuple-element.642) | copy-start | bytes 3076
  114.7 122.5 %copy-start.36 = (f32[1,1,256]{2,1,0:T(1,128)}, f32[1,1,256]{2,1,0:T(1,128)S(1)}, u32[]{:S(2)}) copy-start(f32[1,1,256]{2,1,0:T(1,128)S(1)} %get-tuple-element.643) | copy-start | bytes 3076
  114.7 122.5 %copy-start.38 = (f32[1,1,256]{2,1,0:T(1,128)}, f32[1,1,256]{2,1,0:T(1,128)S(1)}, u32[]{:S(2)}) copy-start(f32[1,1,256]{2,1,0:T(1,128)S(1)} %get-tuple-element.644) | copy-start | bytes 3076
  114.7 122.5 %copy-start.40 = (f32[1,1,256]{2,1,0:T(1,128)}, f32[1,1,256]{2,1,0:T(1,128)S(1)}, u32[]{:S(2)}) copy-start(f32[1,1,256]{2,1,0:T(1,128)S(1)} %get-tuple-element.645) | copy-start | bytes 3076
  114.7 122.5 %copy-start.42 = (f32[1,1,256]{2,1,0:T(1,128)}, f32[1,1,256]{2,1,0:T(1,128)S(1)}, u32[]{:S(2)}) copy-start(f32[1,1,256]{2,1,0:T(1,128)S(1)} %get-tuple-element.646) | copy-start | bytes 3076
  114.7 122.5 %copy-start.44 = (f32[1,1,256]{2,1,0:T(1,128)}, f32[1,1,256]{2,1,0:T(1,128)S(1)}, u32[]{:S(2)}) copy-start(f32[1,1,256]{2,1,0:T(1,128)S(1)} %get-tuple-element.647) | copy-start | bytes 3076
  114.8 122.5 %copy-start.46 = (f32[1,1,256]{2,1,0:T(1,128)}, f32[1,1,256]{2,1,0:T(1,128)S(1)}, u32[]{:S(2)}) copy-start(f32[1,1,256]{2,1,0:T(1,128)S(1)} %get-tuple-element.648) | copy-start | bytes 3076
  264.1 24.0 %copy-start.7 = (f32[16,256]{1,0:T(8,128)S(1)}, f32[16,256]{1,0:T(8,128)}, u32[]{:S(2)}) copy-start(f32[16,256]{1,0:T(8,128)} %get-tuple-element.435) | copy-start | bytes 49156
  310.3 6.7 %copy-start.1 = (f32[256,128]{1,0:T(8,128)S(1)}, f32[256,128]{1,0:T(8,128)}, u32[]{:S(2)}) copy-start(f32[256,128]{1,0:T(8,128)} %reduce-scatter.2.cloned.1.call-done) | copy-start | bytes 393220
  310.3 15.6 %copy-start.35 = (f32[1,1,256]{2,1,0:T(1,128)S(1)}, f32[1,1,256]{2,1,0:T(1,128)}, u32[]{:S(2)}) copy-start(f32[1,1,256]{2,1,0:T(1,128)} %copy-done.34) | copy-start | bytes 3076
  310.3 15.6 %copy-start.37 = (f32[1,1,256]{2,1,0:T(1,128)S(1)}, f32[1,1,256]{2,1,0:T(1,128)}, u32[]{:S(2)}) copy-start(f32[1,1,256]{2,1,0:T(1,128)} %copy-done.36) | copy-start | bytes 3076
  310.3 15.6 %copy-start.39 = (f32[1,1,256]{2,1,0:T(1,128)S(1)}, f32[1,1,256]{2,1,0:T(1,128)}, u32[]{:S(2)}) copy-start(f32[1,1,256]{2,1,0:T(1,128)} %copy-done.38) | copy-start | bytes 3076
  310.3 15.6 %copy-start.41 = (f32[1,1,256]{2,1,0:T(1,128)S(1)}, f32[1,1,256]{2,1,0:T(1,128)}, u32[]{:S(2)}) copy-start(f32[1,1,256]{2,1,0:T(1,128)} %copy-done.40) | copy-start | bytes 3076
  310.3 15.6 %copy-start.43 = (f32[1,1,256]{2,1,0:T(1,128)S(1)}, f32[1,1,256]{2,1,0:T(1,128)}, u32[]{:S(2)}) copy-start(f32[1,1,256]{2,1,0:T(1,128)} %copy-done.42) | copy-start | bytes 3076
  310.4 15.6 %copy-start.45 = (f32[1,1,256]{2,1,0:T(1,128)S(1)}, f32[1,1,256]{2,1,0:T(1,128)}, u32[]{:S(2)}) copy-start(f32[1,1,256]{2,1,0:T(1,128)} %copy-done.44) | copy-start | bytes 3076
  310.4 15.6 %copy-start.47 = (f32[1,1,256]{2,1,0:T(1,128)S(1)}, f32[1,1,256]{2,1,0:T(1,128)}, u32[]{:S(2)}) copy-start(f32[1,1,256]{2,1,0:T(1,128)} %copy-done.46) | copy-start | bytes 3076
  317.1 8.7 %collective-permute-start.1 = (f32[3,6,256]{1,2,0:T(8,128)S(1)}, f32[3,6,256]{1,2,0:T(8,128)S(1)}, u32[]{:S(2)}, u32[]{:S(2)}) collective-permute-start(f32[3,6,256]{1,2,0:T(8,128)S(1)} %pad_maximum_fusion.1), channel_id=1, source_target_pairs={{32,0},{64,32},{96,64},{128,96},{160,128},{192,160},{224,192},{33,... | collective-permute-start | bytes 55304 | tf_op jit(solution)/shard_map/ppermute | solution.py:14
  325.8 28.7 %copy-start.20 = (f32[1,1,256]{2,1,0:T(1,128)S(1)}, f32[1,1,256]{2,1,0:T(1,128)}, u32[]{:S(2)}) copy-start(f32[1,1,256]{2,1,0:T(1,128)} %copy-done.19) | copy-start | bytes 3076
  325.8 28.7 %copy-start.22 = (f32[1,1,256]{2,1,0:T(1,128)S(1)}, f32[1,1,256]{2,1,0:T(1,128)}, u32[]{:S(2)}) copy-start(f32[1,1,256]{2,1,0:T(1,128)} %copy-done.21) | copy-start | bytes 3076
  325.8 28.6 %copy-start.24 = (f32[1,1,256]{2,1,0:T(1,128)S(1)}, f32[1,1,256]{2,1,0:T(1,128)}, u32[]{:S(2)}) copy-start(f32[1,1,256]{2,1,0:T(1,128)} %copy-done.23) | copy-start | bytes 3076
  325.8 28.6 %copy-start.26 = (f32[1,1,256]{2,1,0:T(1,128)S(1)}, f32[1,1,256]{2,1,0:T(1,128)}, u32[]{:S(2)}) copy-start(f32[1,1,256]{2,1,0:T(1,128)} %copy-done.25) | copy-start | bytes 3076
  326.4 30.0 %copy-start.10 = (f32[1,1,256]{2,1,0:T(1,128)S(1)}, f32[1,1,256]{2,1,0:T(1,128)}, u32[]{:S(2)}) copy-start(f32[1,1,256]{2,1,0:T(1,128)} %copy-done.9) | copy-start | bytes 3076
  326.4 30.0 %copy-start.12 = (f32[1,1,256]{2,1,0:T(1,128)S(1)}, f32[1,1,256]{2,1,0:T(1,128)}, u32[]{:S(2)}) copy-start(f32[1,1,256]{2,1,0:T(1,128)} %copy-done.11) | copy-start | bytes 3076
  326.5 29.9 %copy-start.14 = (f32[1,1,256]{2,1,0:T(1,128)S(1)}, f32[1,1,256]{2,1,0:T(1,128)}, u32[]{:S(2)}) copy-start(f32[1,1,256]{2,1,0:T(1,128)} %copy-done.13) | copy-start | bytes 3076
  326.5 29.9 %copy-start.16 = (f32[1,1,256]{2,1,0:T(1,128)S(1)}, f32[1,1,256]{2,1,0:T(1,128)}, u32[]{:S(2)}) copy-start(f32[1,1,256]{2,1,0:T(1,128)} %copy-done.15) | copy-start | bytes 3076
  326.5 29.9 %copy-start.18 = (f32[1,1,256]{2,1,0:T(1,128)S(1)}, f32[1,1,256]{2,1,0:T(1,128)}, u32[]{:S(2)}) copy-start(f32[1,1,256]{2,1,0:T(1,128)} %copy-done.17) | copy-start | bytes 3076
  326.5 29.9 %copy-start.31 = (f32[1,1,256]{2,1,0:T(1,128)S(1)}, f32[1,1,256]{2,1,0:T(1,128)}, u32[]{:S(2)}) copy-start(f32[1,1,256]{2,1,0:T(1,128)} %copy-done.30) | copy-start | bytes 3076
  326.5 29.9 %copy-start.33 = (f32[1,1,256]{2,1,0:T(1,128)S(1)}, f32[1,1,256]{2,1,0:T(1,128)}, u32[]{:S(2)}) copy-start(f32[1,1,256]{2,1,0:T(1,128)} %copy-done.32) | copy-start | bytes 3076
  328.3 75.4 %all-to-all-start = ((bf16[32,128,256]{1,2,0:T(8,128)(2,1)}), bf16[32,128,256]{1,2,0:T(8,128)(2,1)S(1)}, u32[]{:S(2)}, u32[]{:S(2)}) async-start(bf16[32,128,256]{1,2,0:T(8,128)(2,1)} %stack.22), calls=%async_computation.1 | async-start | bytes 4194304 | tf_op jit(solution)/shard_map/all_to_all | solution.py:160
Sparse Core Ops, SparseCore 0:
  9.8 95.8 all-gather.4
  111.3 124.2 reduce-scatter.1
